TPU v7x, 256 devices: a whole 4x4x8 slice. The times are simulated.
256 devices in a mesh: row: 16 (over z_hi, y, core), col: 4 (over z_lo), pblk: 4 (over x).
Axes of the slice: x: 4, y: 4, z: 8 (z_hi: 2, z_lo: 4; z = z_hi * 4 + z_lo), core: 2. Of those that a mesh axis runs over, the one named last changes fastest.
Arguments:
- left_feat: int32 [2048, 256], P(('row', 'col', 'pblk')), may hold values from 0 to 255
- right_feat: int32 [4, 4, 64, 256], P('col', 'pblk', 'row'), may hold values from 0 to 255
- embed: bfloat16 [1024, 256], replicated, may hold values from -12 to 12
- conv_w: bfloat16 [8, 768, 256], replicated, may hold values from -0.01953125 to 0.01953125
- head: float32 [256], replicated, may hold values from -0.078125 to 0.078125
- assign: int32 [8], replicated, may hold values from 0 to 3, as said below
- proj_delta: bfloat16 [4, 256, 128], replicated, may hold values from -0.375 to 0.375
- proj_input: bfloat16 [4, 768, 128], replicated, may hold values from -0.21875 to 0.21875
Outputs:
- kernel: float32 [2048, 1024], P('row', ('col', 'pblk'))
Inputs may be any that keep to these rules, and one draw needn't show every extreme that they name: `assign`: every one of the 4 blocks is named by exactly 2 layers.
All inputs are finite; a program needn't handle non-finite values.
Results may differ from a plain program's by a relative error of at most 0.00036.
Values may be sent and summed in bfloat16 or wider, within the bound.
No kernel may reach another device: no remote copies, remote signals or barrier semaphores. Data moves between devices by JAX's collectives and lax.ppermute only.
A program may use at most 128 MiB of HBM per device.

v0:
```python
import jax
import jax.numpy as jnp
from jax import lax
from jax.sharding import Mesh, PartitionSpec as P

SEQ = 64
NFEAT = 4
VOCAB = 256
LAYERS = 8
PR = 128
PS = 128


def shift_wide(inputs):
    blank = jnp.zeros_like(inputs[:, :1])
    earlier = jnp.concatenate([blank, inputs[:, :-1]], 1)
    later_cells = jnp.concatenate([inputs[:, 1:], blank], 1)
    return jnp.concatenate([earlier, inputs, later_cells], 2)


def panels(features, embed, conv_w, head, assign, proj_delta, proj_input):
    examples = features.shape[0]
    blocks_here = proj_delta.shape[0]
    offsets = jnp.arange(NFEAT, dtype=jnp.int32) * VOCAB
    table_rows = features.reshape(examples, SEQ, NFEAT) + offsets
    table_ids = jnp.arange(NFEAT * VOCAB, dtype=jnp.int32)
    onehot = (table_rows[:, :, 0:1] == table_ids).astype(jnp.bfloat16)
    for field in range(1, NFEAT):
        onehot = onehot + (table_rows[:, :, field : field + 1] == table_ids).astype(jnp.bfloat16)
    hidden = jnp.einsum("esv,vc->esc", onehot, embed, preferred_element_type=jnp.float32)
    wides = []
    pres = []
    for layer in range(LAYERS):
        wide_input = shift_wide(hidden.astype(jnp.bfloat16))
        pre_act = jnp.einsum(
            "esk,kc->esc", wide_input, conv_w[layer], preferred_element_type=jnp.float32
        )
        wides.append(wide_input)
        pres.append(pre_act)
        hidden = hidden + jax.nn.silu(pre_act)
    grad_h = jnp.broadcast_to(head / SEQ, hidden.shape)
    block_ids = jnp.arange(blocks_here, dtype=jnp.int32)
    panel = jnp.zeros((examples, blocks_here, PR, PS), jnp.float32)
    for layer in range(LAYERS - 1, -1, -1):
        pre_act = pres[layer]
        sigmoid_z = jax.nn.sigmoid(pre_act)
        delta_low = (grad_h * sigmoid_z * (1.0 + pre_act * (1.0 - sigmoid_z))).astype(jnp.bfloat16)
        block_pick = (assign[layer] == block_ids).astype(jnp.float32)
        rows_table = jnp.einsum("b,bcr->cr", block_pick, proj_delta.astype(jnp.float32)).astype(
            jnp.bfloat16
        )
        cols_table = jnp.einsum("b,bkt->kt", block_pick, proj_input.astype(jnp.float32)).astype(
            jnp.bfloat16
        )
        left_side = jnp.einsum(
            "esc,cr->esr", delta_low, rows_table, preferred_element_type=jnp.float32
        )
        right_side = jnp.einsum(
            "esk,kt->est", wides[layer], cols_table, preferred_element_type=jnp.float32
        )
        projected = jnp.einsum(
            "esr,est->ert", left_side, right_side, precision=lax.Precision.HIGHEST
        )
        panel = panel + block_pick[None, :, None, None] * projected[:, None]
        if layer > 0:
            back_wide = jnp.einsum(
                "esc,kc->esk", delta_low, conv_w[layer], preferred_element_type=jnp.float32
            )
            width = grad_h.shape[2]
            first_third = back_wide[:, :, :width]
            last_third = back_wide[:, :, 2 * width :]
            blank = jnp.zeros_like(first_third[:, :1])
            grad_input = back_wide[:, :, width : 2 * width]
            grad_input = grad_input + jnp.concatenate([first_third[:, 1:], blank], 1)
            grad_input = grad_input + jnp.concatenate([blank, last_third[:, :-1]], 1)
            grad_h = grad_h + grad_input
    return panel.reshape(examples, blocks_here, PR * PS).astype(jnp.bfloat16)


def on_device(left_feat, right_feat, embed, conv_w, head, assign, proj_delta, proj_input):
    group = ("zh", "core", "col")
    n_group = lax.axis_size(group)
    n_zh = lax.axis_size("zh")
    n_core = lax.axis_size("core")
    n_col = lax.axis_size("col")
    n_y = lax.axis_size("y")
    n_blk = lax.axis_size("pblk")
    left_each = left_feat.shape[0]
    right_each = right_feat.shape[2]
    right_local = right_feat.reshape(right_each, right_feat.shape[3])
    own_features = jnp.concatenate([left_feat, right_local], 0)
    panel = panels(own_features, embed, conv_w, head, assign, proj_delta, proj_input)
    own = panel.shape[0]
    width = panel.shape[1] * panel.shape[2] // n_group
    sliced = panel.reshape(own, n_group, width)
    spread = lax.all_to_all(sliced, group, split_axis=1, concat_axis=0, tiled=True)
    spread = spread.reshape(n_group, own, width)
    left_part = spread[:, :left_each].reshape(n_group * left_each, width)
    right_part = spread[:, left_each:].reshape(n_group * right_each, width)
    left_tile = lax.all_gather(left_part, "pblk", axis=0, tiled=True)
    right_tile = lax.all_gather(right_part, "y", axis=0, tiled=True)
    partial_tile = jnp.einsum(
        "lk,rk->lr", left_tile, right_tile, preferred_element_type=jnp.float32
    )
    partial_tile = partial_tile.reshape(
        n_blk, n_zh, n_core, n_col, left_each, n_y, n_zh, n_core, n_col, right_each
    )
    chunks = jnp.transpose(partial_tile, (1, 2, 8, 3, 0, 4, 6, 5, 7, 9))
    chunks = chunks.reshape(n_group, n_col * n_blk * left_each, n_zh * n_y * n_core * right_each)
    block = lax.psum_scatter(chunks, group, scatter_dimension=0, tiled=True)
    return block.reshape(block.shape[1], block.shape[2])


def solution(mesh):
    n_row = mesh.shape["row"]
    fine = Mesh(
        mesh.devices.reshape(2, 4, n_row // 8, mesh.shape["col"], mesh.shape["pblk"]),
        ("zh", "y", "core", "col", "pblk"),
    )
    rows = ("zh", "y", "core")
    placed = (
        P((*rows, "col", "pblk"), None),
        P("col", "pblk", rows, None),
        P(),
        P(),
        P(),
        P(),
        P(),
        P(),
    )
    return jax.shard_map(
        on_device, mesh=fine, in_specs=placed, out_specs=P(rows, ("col", "pblk")), check_vma=False
    )
```

profile of v0, /device:TPU:1, one launch (start us, length us, event | category | flops | bytes accessed | tf_op | source)
XLA Modules:
  0.0 414.9 jit_solution(5127504593989071444)
XLA Ops:
  6.5 1.6 fusion.261
  9.4 1.2 copy.43
  10.6 0.8 fusion.161
  11.4 1.0 fusion.165
  13.0 0.8 fusion.169
  13.8 0.7 fusion.194
  14.5 1.0 fusion.173
  15.5 0.7 fusion.195
  16.2 1.0 fusion.177
  17.8 0.9 fusion.181
  19.3 0.9 fusion.185
  20.8 0.9 fusion.189
  22.4 1.9 fusion.159
  24.2 2.0 fusion.163
  26.2 1.9 fusion.167
  28.1 2.0 fusion.171
  30.1 2.0 fusion.175
  32.1 1.2 fusion.179
  33.3 1.2 fusion.183
  34.5 1.2 fusion.187
  37.8 2.8 fusion.262
  41.3 1.4 copy-done.2
  53.6 1.4 fusion.263
  56.3 0.9 fusion.69
  57.5 1.4 fusion.264
  61.1 1.4 fusion.265
  62.6 1.6 copy.65
  65.6 1.4 fusion.266
  67.1 1.6 copy.66
  70.0 1.4 fusion.267
  71.6 1.6 copy.67
  74.7 1.4 fusion.268
  76.2 1.6 copy.68
  79.2 1.4 fusion.269
  80.7 1.6 copy.69
  83.0 1.4 fusion.270
  85.2 2.4 mul.370
  87.6 5.2 %mul.371 = f32[12,16,4096]{2,1,0:T(8,128)} reshape(f32[12,4,16384]{2,1,0:T(4,128)} %mul.370) | data formatting | bytes 6291456 | tf_op jit(solution)/shard_map/mul | solution.py:64
  92.8 3.7 mul.360
  96.5 5.2 %mul.361 = f32[12,16,4096]{2,1,0:T(8,128)} reshape(f32[12,4,16384]{2,1,0:T(4,128)} %mul.360) | data formatting | bytes 6291456 | tf_op jit(solution)/shard_map/mul | solution.py:64
  101.7 3.7 mul.350
  105.4 5.4 %mul.351 = f32[12,16,4096]{2,1,0:T(8,128)} reshape(f32[12,4,16384]{2,1,0:T(4,128)} %mul.350) | data formatting | bytes 6291456 | tf_op jit(solution)/shard_map/mul | solution.py:64
  110.8 3.6 mul.340
  114.4 5.3 %mul.341 = f32[12,16,4096]{2,1,0:T(8,128)} reshape(f32[12,4,16384]{2,1,0:T(4,128)} %mul.340) | data formatting | bytes 6291456 | tf_op jit(solution)/shard_map/mul | solution.py:64
  119.7 3.6 mul.330
  123.3 5.3 %mul.331 = f32[12,16,4096]{2,1,0:T(8,128)} reshape(f32[12,4,16384]{2,1,0:T(4,128)} %mul.330) | data formatting | bytes 6291456 | tf_op jit(solution)/shard_map/mul | solution.py:64
  128.6 3.7 mul.320
  132.2 5.2 %mul.321 = f32[12,16,4096]{2,1,0:T(8,128)} reshape(f32[12,4,16384]{2,1,0:T(4,128)} %mul.320) | data formatting | bytes 6291456 | tf_op jit(solution)/shard_map/mul | solution.py:64
  137.5 2.4 mul.310
  139.9 5.2 %mul.311 = f32[12,16,4096]{2,1,0:T(8,128)} reshape(f32[12,4,16384]{2,1,0:T(4,128)} %mul.310) | data formatting | bytes 6291456 | tf_op jit(solution)/shard_map/mul | solution.py:64
  145.2 2.4 mul.300
  147.5 5.3 %mul.301 = f32[12,16,4096]{2,1,0:T(8,128)} reshape(f32[12,4,16384]{2,1,0:T(4,128)} %mul.300) | data formatting | bytes 6291456 | tf_op jit(solution)/shard_map/mul | solution.py:64
  152.8 9.6 %add_convert_fusion = bf16[12,16,4096]{2,1,0:T(8,128)(2,1)S(1)} fusion(f32[12,16,4096]{2,1,0:T(8,128)} %mul.371, f32[12,16,4096]{2,1,0:T(8,128)} %mul.361, f32[12,16,4096]{2,1,0:T(8,128)} %mul.351, f32[12,16,4096]{2,1,0:T(8,128)} %mul.341, f32[12,16,4096]{2,1,0:T(8,128)} %mul.331, f32[12,16,4096]{2,1,0:T(8,128)} %mul.321, f32[12,16,4096]{2,1,0:T(8,128)} %mul.311, ...), kind=kLoop, calls=%fused_computation | loop fusion | flops 12582912 | bytes 26739200 | tf_op jit(solution)/shard_map/convert_element_type | solution.py:77
  162.4 0.9 copy.40
  163.3 57.9 %all_to_all.15 = bf16[12,16,4096]{2,0,1:T(8,128)(2,1)S(1)} all-to-all(bf16[12,16,4096]{2,0,1:T(8,128)(2,1)S(1)} %copy.40), channel_id=1, replica_groups=mesh['zh'=2,'y'=4,'core'=2,'col'=4,'pblk'=4] {'zh','core','col'}, dimensions={1} | all-to-all | bytes 3145728 | tf_op jit(solution)/shard_map/all_to_all | solution.py:96
  221.5 1.0 reshape.112
  222.5 1.0 slice_bitcast_fusion
  223.6 31.7 %all-gather.5.cloned.1.call-done = bf16[256,4096]{1,0:T(8,128)(2,1)} async-done(((bf16[64,4096]{1,0:T(8,128)(2,1)}), bf16[256,4096]{1,0:T(8,128)(2,1)}) %all-gather.5.cloned.1.call-update) | async-done | bytes 2097168 | tf_op jit(solution)/shard_map/all_gather | solution.py:101
  255.3 52.6 %all-gather.3.cloned.1.call-done = bf16[512,4096]{1,0:T(8,128)(2,1)} async-done(((bf16[128,4096]{1,0:T(8,128)(2,1)}), bf16[512,4096]{1,0:T(8,128)(2,1)}) %all-gather.3.cloned.1.call-update) | async-done | bytes 4194320 | tf_op jit(solution)/shard_map/all_gather | solution.py:100
  307.9 4.2 %fusion.271 = f32[512,256]{0,1:T(8,128)S(1)} fusion(bf16[512,4096]{1,0:T(8,128)(2,1)} %all-gather.3.cloned.1.call-done, bf16[256,4096]{1,0:T(8,128)(2,1)} %all-gather.5.cloned.1.call-done), kind=kOutput, calls=%fused_computation.291 | convolution fusion | flops 1073741824 | bytes 6815744 | tf_op jit(solution)/shard_map/lk,rk->lr/dot_general | solution.py:102
  312.1 11.5 %reshape.113 = f32[4,2,2,4,8,4,2,2,4,4]{4,3,2,1,0,9,8,7,6,5:T(4,128)} reshape(f32[512,256]{0,1:T(8,128)S(1)} %fusion.271) | data formatting | bytes 1048576 | tf_op jit(solution)/shard_map/reshape | solution.py:105
  323.6 9.9 %copy.42 = f32[2,2,4,4,4,8,2,4,2,4]{5,4,3,9,8,7,6,2,1,0:T(4,128)} copy(f32[2,2,4,4,4,8,2,4,2,4]{5,3,1,0,4,9,2,8,6,7:T(4,128)} %bitcast.292) | data formatting | bytes 1048576 | tf_op jit(solution)/shard_map/transpose | solution.py:108
  333.5 11.1 %reshape.114 = f32[16,128,64]{1,2,0:T(8,128)} reshape(f32[2,2,4,4,4,8,2,4,2,4]{5,4,3,9,8,7,6,2,1,0:T(4,128)} %copy.42) | data formatting | bytes 1048576 | tf_op jit(solution)/shard_map/reshape | solution.py:109
  344.6 63.3 %reduce-scatter.2.cloned.1.call-done = f32[1,128,64]{1,2,0:T(8,128)} async-done(((f32[16,128,64]{1,2,0:T(8,128)}), f32[1,128,64]{1,2,0:T(8,128)}) %reduce-scatter.2.cloned.1.call-update) | async-done | bytes 32784 | tf_op jit(solution)/shard_map/reduce_scatter | solution.py:110
  (125 shorter events, 29.1 us)
Async XLA Ops:
  6.5 31.3 %copy-start = (bf16[1024,256]{1,0:T(8,128)(2,1)S(1)}, bf16[1024,256]{1,0:T(8,128)(2,1)}, u32[]{:S(2)}) copy-start(bf16[1024,256]{1,0:T(8,128)(2,1)} %param.10) | copy-start | bytes 1572868
  6.5 15.2 %copy-start.3 = (bf16[4,768,128]{2,1,0:T(8,128)(2,1)S(1)}, bf16[4,768,128]{2,1,0:T(8,128)(2,1)}, u32[]{:S(2)}) copy-start(bf16[4,768,128]{2,1,0:T(8,128)(2,1)} %param.15) | copy-start | bytes 2359300
  6.5 248.8 %all-gather.5.cloned.1.call-start = ((), (), s32[]{:S(2)}) async-start(), calls=%async_computation.3 | async-start | bytes 2621440 | tf_op jit(solution)/shard_map/all_gather | solution.py:101
  32.1 3.6 copy-start.6
  32.1 4.8 %copy-start.4 = (s32[8,256]{1,0:T(8,128)S(1)}, s32[8,256]{1,0:T(8,128)}, u32[]{:S(2)}) copy-start(s32[8,256]{1,0:T(8,128)} %param.8) | copy-start | bytes 24580
  32.1 5.0 %copy-start.5 = (s32[1,1,4,256]{3,2,1,0:T(4,128)S(1)}, s32[1,1,4,256]{3,2,1,0:T(4,128)}, u32[]{:S(2)}) copy-start(s32[1,1,4,256]{3,2,1,0:T(4,128)} %param.9) | copy-start | bytes 12292
  37.8 3.0 copy-start.11
  40.8 1.9 copy-start.2
  42.7 1.0 copy-start.10
  44.2 1.0 copy-start.9
  45.6 1.0 copy-start.8
  47.1 1.0 copy-start.7
  222.5 85.5 %all-gather.3.cloned.1.call-start = ((), (), s32[]{:S(2)}) async-start(), calls=%async_computation.2 | async-start | bytes 5242880 | tf_op jit(solution)/shard_map/all_gather | solution.py:100
  223.6 184.3 %reduce-scatter.2.cloned.1.call-start = ((), (), s32[]{:S(2)}) async-start(), calls=%async_computation.4 | async-start | bytes 557056 | tf_op jit(solution)/shard_map/reduce_scatter | solution.py:110
  333.5 74.4 %copy-start.1 = (bf16[1024,256]{1,0:T(8,128)(2,1)S(1)}, bf16[1024,256]{1,0:T(8,128)(2,1)}, u32[]{:S(2)}) copy-start(bf16[1024,256]{1,0:T(8,128)(2,1)} %param.10) | copy-start | bytes 1572868
Sparse Core Ops, SparseCore 0:
  222.6 32.7 all-gather.4
  257.1 50.7 all-gather.2
  344.8 63.1 reduce-scatter.1
where the time goes:
time: 422 us; the launch traced here: 415 us
  waiting for transfers between devices  148 us (35%)
  local copies, waits for them, and re-layouts  124 us (29%)
  blocking collectives  57.9 us (14%)
  matrix products  53.7 us (13%)
  other arithmetic  17.5 us (4%)
  between operations  14.3 us (3%)
    mul x32, local copies, waits for them, and re-layouts, panels(): panel = panel + block_pick[None, :, None, None] * projected[:, None]  68.9 us
    reduce_scatter x1, waiting for transfers between devices, on_device(): block = lax.psum_scatter(chunks, group, scatter_dimension=0, tiled=True)  63.3 us
    all_to_all x1, blocking collectives, on_device(): lax.all_to_all(sliced, group, split_axis=1, concat_axis=0, tiled=True)  57.9 us
    all_gather x1, waiting for transfers between devices, on_device(): left_tile = lax.all_gather(left_part, 'pblk', axis=0, tiled=True)  52.6 us
    all_gather x1, waiting for transfers between devices, on_device(): right_tile = lax.all_gather(right_part, 'y', axis=0, tiled=True)  31.7 us
    unnamed x43, local copies, waits for them, and re-layouts  14.8 us
    dot_general x8, matrix products, panels(): jnp.einsum('b,bkt->kt', block_pick, proj_input.astype(jnp.float32))  13.3 us
    reshape x1, local copies, waits for them, and re-layouts, on_device(): partial_tile.reshape(n_blk, n_zh, n_core, n_col, left_each, n_y, n_zh, n_...  11.5 us
  transfers between devices with their start and end apart: 3, of which 3 were waited for; matrix products, arithmetic and copies ran while one was open for 0% of the time, Pallas kernels for 0%

commit v1 on v0

--- a/solution.py
+++ b/solution.py
@@ -9,6 +9,21 @@
 LAYERS = 8
 PR = 128
 PS = 128
+
+
+def ring_apply(array, axis, dim, make, out_dim):
+    ways, here, lap = (lax.axis_size(axis), lax.axis_index(axis), array.shape[dim])
+    results = []
+    for far in range(ways):
+        arriving = (
+            lax.ppermute(array, axis, [(d, (d + 1) % ways) for d in range(ways)])
+            if far + 1 < ways
+            else array
+        )
+        results.append(make(array, (here - far) % ways * lap))
+        array = arriving
+    line = jnp.concatenate(results[::-1], axis=out_dim)
+    return jnp.roll(line, (here + 1) * results[0].shape[out_dim], axis=out_dim)
 
 
 def shift_wide(inputs):
@@ -97,10 +112,15 @@
     spread = spread.reshape(n_group, own, width)
     left_part = spread[:, :left_each].reshape(n_group * left_each, width)
     right_part = spread[:, left_each:].reshape(n_group * right_each, width)
-    left_tile = lax.all_gather(left_part, "pblk", axis=0, tiled=True)
     right_tile = lax.all_gather(right_part, "y", axis=0, tiled=True)
-    partial_tile = jnp.einsum(
-        "lk,rk->lr", left_tile, right_tile, preferred_element_type=jnp.float32
+    partial_tile = ring_apply(
+        left_part,
+        "pblk",
+        0,
+        lambda shard, start: jnp.einsum(
+            "lk,rk->lr", shard, right_tile, preferred_element_type=jnp.float32
+        ),
+        0,
     )
     partial_tile = partial_tile.reshape(
         n_blk, n_zh, n_core, n_col, left_each, n_y, n_zh, n_core, n_col, right_each

time: 422 us -> 422 us (level)
  matrix products: 53.7 us -> 69.2 us
  waiting for transfers between devices: 148 us -> 136 us
  local copies, waits for them, and re-layouts: 124 us -> 116 us
    ppermute x0 -> x3, waiting for transfers between devices: none -> 72.6 us  [ring_apply(): lax.ppermute(array, axis, [(d, (d + 1) % ways) for d in range(ways)])]
    all_gather x1 -> x0, waiting for transfers between devices: 52.6 us -> none  [on_device(): left_tile = lax.all_gather(left_part, 'pblk', axis=0, tiled=True)]
    all_gather x1, waiting for transfers between devices: 31.7 us -> 0.01 us  [on_device(): right_tile = lax.all_gather(right_part, 'y', axis=0, tiled=True)]
    dot_general x8, matrix products: 3.85 us -> 9.74 us  [panels(): jnp.einsum('esk,kt->est', wides[layer], cols_table, preferred_element_typ...]
    mul x32, local copies, waits for them, and re-layouts: 68.9 us -> 63.4 us  [panels(): panel = panel + block_pick[None, :, None, None] * projected[:, None]]
    unnamed x43 -> x126, local copies, waits for them, and re-layouts: 14.8 us -> 12 us
  transfers between devices with their start and end apart: 3 -> 5, of which waited for: 3 -> 4; matrix products, arithmetic and copies ran while one was open for 0% -> 0% of each run, Pallas kernels for 0% -> 0%
where the time goes in v1:
time: 422 us; the launch traced here: 415 us
  waiting for transfers between devices  136 us (32%)
  local copies, waits for them, and re-layouts  116 us (27%)
  matrix products  69.2 us (16%)
  blocking collectives  57.9 us (14%)
  other arithmetic  19.4 us (5%)
  between operations  14.9 us (4%)
    ppermute x3, waiting for transfers between devices, ring_apply(): lax.ppermute(array, axis, [(d, (d + 1) % ways) for d in range(ways)])  72.6 us
    reduce_scatter x1, waiting for transfers between devices, on_device(): block = lax.psum_scatter(chunks, group, scatter_dimension=0, tiled=True)  63.5 us
    mul x32, local copies, waits for them, and re-layouts, panels(): panel = panel + block_pick[None, :, None, None] * projected[:, None]  63.4 us
    all_to_all x1, blocking collectives, on_device(): lax.all_to_all(sliced, group, split_axis=1, concat_axis=0, tiled=True)  57.9 us
    dot_general x8, matrix products, panels(): jnp.einsum('b,bkt->kt', block_pick, proj_input.astype(jnp.float32))  15.3 us
    unnamed x126, local copies, waits for them, and re-layouts  12 us
    dot_general x8, matrix products, panels(): jnp.einsum('esr,est->ert', left_side, right_side, precision=lax.Precision...  11.3 us
    reshape x1, local copies, waits for them, and re-layouts, on_device(): partial_tile.reshape(n_blk, n_zh, n_core, n_col, left_each, n_y, n_zh, n_...  11.3 us
  transfers between devices with their start and end apart: 5, of which 4 were waited for; matrix products, arithmetic and copies ran while one was open for 0% of the time, Pallas kernels for 0%

profile of v1, /device:TPU:1, one launch (start us, length us, event | category | flops | bytes accessed | tf_op | source)
XLA Modules:
  0.0 414.6 jit_solution(7836536822213073132)
XLA Ops:
  6.5 1.2 copy.42
  7.8 1.6 fusion.262
  9.4 1.7 copy.44
  11.1 1.5 fusion.161
  12.7 1.9 fusion.159
  14.6 1.5 fusion.165
  16.1 1.9 fusion.163
  17.9 1.5 fusion.169
  19.5 1.9 fusion.167
  21.4 1.6 fusion.173
  23.0 2.0 fusion.171
  25.0 1.5 fusion.177
  26.5 1.8 fusion.175
  28.3 1.5 fusion.181
  29.8 1.9 fusion.179
  32.7 2.0 fusion.183
  35.6 1.9 fusion.187
  37.5 1.2 fusion.191
  39.8 1.1 fusion.193
  40.9 1.2 fusion.194
  45.4 2.8 fusion.263
  66.5 1.4 fusion.271
  68.6 2.4 mul.373
  71.0 5.2 %mul.374 = f32[12,16,4096]{2,1,0:T(8,128)} reshape(f32[12,4,16384]{2,1,0:T(4,128)} %mul.373) | data formatting | bytes 6291456 | tf_op jit(solution)/shard_map/mul | solution.py:79
  76.5 1.8 fusion.114
  78.4 1.4 fusion.270
  80.5 2.5 mul.363
  83.0 5.3 %mul.364 = f32[12,16,4096]{2,1,0:T(8,128)} reshape(f32[12,4,16384]{2,1,0:T(4,128)} %mul.363) | data formatting | bytes 6291456 | tf_op jit(solution)/shard_map/mul | solution.py:79
  88.5 1.7 fusion.116
  90.2 1.4 fusion.269
  92.3 2.5 mul.353
  94.8 5.4 %mul.354 = f32[12,16,4096]{2,1,0:T(8,128)} reshape(f32[12,4,16384]{2,1,0:T(4,128)} %mul.353) | data formatting | bytes 6291456 | tf_op jit(solution)/shard_map/mul | solution.py:79
  100.6 1.7 fusion.118
  102.3 1.4 fusion.268
  104.4 2.4 mul.343
  106.8 5.3 %mul.344 = f32[12,16,4096]{2,1,0:T(8,128)} reshape(f32[12,4,16384]{2,1,0:T(4,128)} %mul.343) | data formatting | bytes 6291456 | tf_op jit(solution)/shard_map/mul | solution.py:79
  112.4 1.6 fusion.120
  114.0 1.4 fusion.267
  116.2 2.4 mul.333
  118.5 5.3 %mul.334 = f32[12,16,4096]{2,1,0:T(8,128)} reshape(f32[12,4,16384]{2,1,0:T(4,128)} %mul.333) | data formatting | bytes 6291456 | tf_op jit(solution)/shard_map/mul | solution.py:79
  124.2 1.5 fusion.122
  125.6 1.4 fusion.266
  127.8 2.4 mul.323
  130.2 5.5 %mul.324 = f32[12,16,4096]{2,1,0:T(8,128)} reshape(f32[12,4,16384]{2,1,0:T(4,128)} %mul.323) | data formatting | bytes 6291456 | tf_op jit(solution)/shard_map/mul | solution.py:79
  136.5 1.4 fusion.265
  138.6 2.5 mul.313
  141.1 5.3 %mul.314 = f32[12,16,4096]{2,1,0:T(8,128)} reshape(f32[12,4,16384]{2,1,0:T(4,128)} %mul.313) | data formatting | bytes 6291456 | tf_op jit(solution)/shard_map/mul | solution.py:79
  147.2 1.4 fusion.264
  149.3 2.4 mul.303
  151.7 5.3 %mul.304 = f32[12,16,4096]{2,1,0:T(8,128)} reshape(f32[12,4,16384]{2,1,0:T(4,128)} %mul.303) | data formatting | bytes 6291456 | tf_op jit(solution)/shard_map/mul | solution.py:79
  158.3 9.6 %add_convert_fusion = bf16[12,16,4096]{2,1,0:T(8,128)(2,1)S(1)} fusion(f32[12,16,4096]{2,1,0:T(8,128)} %mul.374, f32[12,16,4096]{2,1,0:T(8,128)} %mul.364, f32[12,16,4096]{2,1,0:T(8,128)} %mul.354, f32[12,16,4096]{2,1,0:T(8,128)} %mul.344, f32[12,16,4096]{2,1,0:T(8,128)} %mul.334, f32[12,16,4096]{2,1,0:T(8,128)} %mul.324, f32[12,16,4096]{2,1,0:T(8,128)} %mul.314, ...), kind=kLoop, calls=%fused_computation | loop fusion | flops 12582912 | bytes 26739200 | tf_op jit(solution)/shard_map/convert_element_type | solution.py:92
  168.8 57.9 %all_to_all.15 = bf16[12,16,4096]{2,0,1:T(8,128)(2,1)S(1)} all-to-all(bf16[12,16,4096]{2,0,1:T(8,128)(2,1)S(1)} %copy.39), channel_id=1, replica_groups=mesh['zh'=2,'y'=4,'core'=2,'col'=4,'pblk'=4] {'zh','core','col'}, dimensions={1} | all-to-all | bytes 3145728 | tf_op jit(solution)/shard_map/all_to_all | solution.py:111
  226.7 1.1 slice_bitcast_fusion
  227.8 1.2 collective-permute-start
  230.3 23.4 %collective-permute-done = bf16[128,4096]{1,0:T(8,128)(2,1)} collective-permute-done((bf16[128,4096]{1,0:T(8,128)(2,1)}, bf16[128,4096]{1,0:T(8,128)(2,1)}, u32[]{:S(2)}, u32[]{:S(2)}) %collective-permute-start) | collective-permute-done | bytes 1048608 | tf_op jit(solution)/shard_map/ppermute | solution.py:19
  253.9 25.0 %collective-permute-done.1 = bf16[128,4096]{1,0:T(8,128)(2,1)} collective-permute-done((bf16[128,4096]{1,0:T(8,128)(2,1)}, bf16[128,4096]{1,0:T(8,128)(2,1)}, u32[]{:S(2)}, u32[]{:S(2)}) %collective-permute-start.1) | collective-permute-done | bytes 1048608 | tf_op jit(solution)/shard_map/ppermute | solution.py:19
  278.9 24.1 %collective-permute-done.2 = bf16[128,4096]{1,0:T(8,128)(2,1)} collective-permute-done((bf16[128,4096]{1,0:T(8,128)(2,1)}, bf16[128,4096]{1,0:T(8,128)(2,1)}, u32[]{:S(2)}, u32[]{:S(2)}) %collective-permute-start.2) | collective-permute-done | bytes 1048608 | tf_op jit(solution)/shard_map/ppermute | solution.py:19
  303.1 2.9 constant_dynamic-update-slice_fusion.7
  306.0 2.1 constant_dynamic-update-slice_fusion.6
  308.1 2.1 constant_dynamic-update-slice_fusion.5
  311.4 11.3 %reshape.113 = f32[4,2,2,4,8,4,2,2,4,4]{4,3,2,1,0,9,8,7,6,5:T(4,128)} reshape(f32[512,256]{0,1:T(8,128)S(1)} %copy.40) | data formatting | bytes 1048576 | tf_op jit(solution)/shard_map/reshape | solution.py:125
  322.7 10.0 %copy.41 = f32[2,2,4,4,4,8,2,4,2,4]{5,4,3,9,8,7,6,2,1,0:T(4,128)} copy(f32[2,2,4,4,4,8,2,4,2,4]{5,3,1,0,4,9,2,8,6,7:T(4,128)} %bitcast.300) | data formatting | bytes 1048576 | tf_op jit(solution)/shard_map/transpose | solution.py:128
  332.7 11.1 %reshape.114 = f32[16,128,64]{1,2,0:T(8,128)} reshape(f32[2,2,4,4,4,8,2,4,2,4]{5,4,3,9,8,7,6,2,1,0:T(4,128)} %copy.41) | data formatting | bytes 1048576 | tf_op jit(solution)/shard_map/reshape | solution.py:129
  343.8 63.5 %reduce-scatter.2.cloned.1.call-done = f32[1,128,64]{1,2,0:T(8,128)} async-done(((f32[16,128,64]{1,2,0:T(8,128)}), f32[1,128,64]{1,2,0:T(8,128)}) %reduce-scatter.2.cloned.1.call-update) | async-done | bytes 32784 | tf_op jit(solution)/shard_map/reduce_scatter | solution.py:130
  (217 shorter events, 37.2 us)
Async XLA Ops:
  6.5 38.9 %copy-start = (bf16[1024,256]{1,0:T(8,128)(2,1)S(1)}, bf16[1024,256]{1,0:T(8,128)(2,1)}, u32[]{:S(2)}) copy-start(bf16[1024,256]{1,0:T(8,128)(2,1)} %param.10) | copy-start | bytes 1572868
  6.5 296.5 %all-gather.2.cloned.1.call-start = ((), (), s32[]{:S(2)}) async-start(), calls=%async_computation.2 | async-start | bytes 2621440 | tf_op jit(solution)/shard_map/all_gather | solution.py:115
  31.6 12.9 %copy-start.42 = (s32[1,1,4,256]{3,2,1,0:T(4,128)S(1)}, s32[1,1,4,256]{3,2,1,0:T(4,128)}, u32[]{:S(2)}) copy-start(s32[1,1,4,256]{3,2,1,0:T(4,128)} %param.9) | copy-start | bytes 12292
  31.6 13.1 %copy-start.41 = (s32[8,256]{1,0:T(8,128)S(1)}, s32[8,256]{1,0:T(8,128)}, u32[]{:S(2)}) copy-start(s32[8,256]{1,0:T(8,128)} %param.8) | copy-start | bytes 24580
  45.4 3.0 copy-start.3
  48.9 0.8 copy-start.14
  49.1 0.8 copy-start.34
  49.1 0.9 copy-start.35
  50.0 0.7 copy-start.12
  50.1 0.7 copy-start.32
  50.1 0.9 copy-start.33
  51.0 0.8 copy-start.10
  51.2 0.7 copy-start.30
  51.2 0.9 copy-start.31
  52.1 0.7 copy-start.8
  52.2 0.8 copy-start.27
  52.2 0.9 copy-start.29
  53.1 0.9 copy-start.6
  53.2 0.7 copy-start.23
  53.2 0.9 copy-start.25
  53.2 1.0 copy-start.43
  54.1 0.7 copy-start.4
  54.2 0.8 copy-start.19
  54.3 1.0 copy-start.21
  55.3 0.8 copy-start.15
  55.3 0.9 copy-start.17
  63.6 1.0 copy-start.50
  64.6 0.9 copy-start.51
  71.0 5.2 %copy-start.40 = (f32[1,256,128]{2,0,1:T(1,128)S(1)}, f32[1,256,128]{2,0,1:T(1,128)}, u32[]{:S(2)}) copy-start(f32[1,256,128]{2,0,1:T(1,128)} %fusion.165) | copy-start | bytes 393220
  83.0 5.3 %copy-start.39 = (f32[1,256,128]{2,0,1:T(1,128)S(1)}, f32[1,256,128]{2,0,1:T(1,128)}, u32[]{:S(2)}) copy-start(f32[1,256,128]{2,0,1:T(1,128)} %fusion.169) | copy-start | bytes 393220
  83.0 5.5 %copy-start.13 = (bf16[12,64,256]{2,1,0:T(8,128)(2,1)S(1)}, bf16[12,64,256]{2,1,0:T(8,128)(2,1)}, u32[]{:S(2)}) copy-start(bf16[12,64,256]{2,1,0:T(8,128)(2,1)} %copy-done.12) | copy-start | bytes 1179652
  94.8 5.5 %copy-start.38 = (f32[1,256,128]{2,0,1:T(1,128)S(1)}, f32[1,256,128]{2,0,1:T(1,128)}, u32[]{:S(2)}) copy-start(f32[1,256,128]{2,0,1:T(1,128)} %fusion.173) | copy-start | bytes 393220
  94.8 5.7 %copy-start.11 = (bf16[12,64,256]{2,1,0:T(8,128)(2,1)S(1)}, bf16[12,64,256]{2,1,0:T(8,128)(2,1)}, u32[]{:S(2)}) copy-start(bf16[12,64,256]{2,1,0:T(8,128)(2,1)} %copy-done.10) | copy-start | bytes 1179652
  106.8 5.3 %copy-start.37 = (f32[1,256,128]{2,0,1:T(1,128)S(1)}, f32[1,256,128]{2,0,1:T(1,128)}, u32[]{:S(2)}) copy-start(f32[1,256,128]{2,0,1:T(1,128)} %fusion.177) | copy-start | bytes 393220
  106.8 5.6 %copy-start.9 = (bf16[12,64,256]{2,1,0:T(8,128)(2,1)S(1)}, bf16[12,64,256]{2,1,0:T(8,128)(2,1)}, u32[]{:S(2)}) copy-start(bf16[12,64,256]{2,1,0:T(8,128)(2,1)} %copy-done.8) | copy-start | bytes 1179652
  106.8 5.6 %copy-start.28 = (bf16[12,63,256]{2,1,0:T(8,128)(2,1)S(1)}, bf16[12,63,256]{2,1,0:T(8,128)(2,1)}, u32[]{:S(2)}) copy-start(bf16[12,63,256]{2,1,0:T(8,128)(2,1)} %copy-done.27) | copy-start | bytes 1161220
  118.5 5.3 %copy-start.36 = (f32[1,256,128]{2,0,1:T(1,128)S(1)}, f32[1,256,128]{2,0,1:T(1,128)}, u32[]{:S(2)}) copy-start(f32[1,256,128]{2,0,1:T(1,128)} %fusion.181) | copy-start | bytes 393220
  118.5 5.6 %copy-start.7 = (bf16[12,64,256]{2,1,0:T(8,128)(2,1)S(1)}, bf16[12,64,256]{2,1,0:T(8,128)(2,1)}, u32[]{:S(2)}) copy-start(bf16[12,64,256]{2,1,0:T(8,128)(2,1)} %copy-done.6) | copy-start | bytes 1179652
  118.5 5.6 %copy-start.24 = (bf16[12,63,256]{2,1,0:T(8,128)(2,1)S(1)}, bf16[12,63,256]{2,1,0:T(8,128)(2,1)}, u32[]{:S(2)}) copy-start(bf16[12,63,256]{2,1,0:T(8,128)(2,1)} %copy-done.23) | copy-start | bytes 1161220
  118.5 5.6 %copy-start.26 = (bf16[12,63,256]{2,1,0:T(8,128)(2,1)S(1)}, bf16[12,63,256]{2,1,0:T(8,128)(2,1)}, u32[]{:S(2)}) copy-start(bf16[12,63,256]{2,1,0:T(8,128)(2,1)} %copy-done.25) | copy-start | bytes 1161220
  130.2 5.8 %copy-start.5 = (bf16[12,64,256]{2,1,0:T(8,128)(2,1)S(1)}, bf16[12,64,256]{2,1,0:T(8,128)(2,1)}, u32[]{:S(2)}) copy-start(bf16[12,64,256]{2,1,0:T(8,128)(2,1)} %copy-done.4) | copy-start | bytes 1179652
  130.2 5.8 %copy-start.20 = (bf16[12,63,256]{2,1,0:T(8,128)(2,1)S(1)}, bf16[12,63,256]{2,1,0:T(8,128)(2,1)}, u32[]{:S(2)}) copy-start(bf16[12,63,256]{2,1,0:T(8,128)(2,1)} %copy-done.19) | copy-start | bytes 1161220
  130.2 5.8 %copy-start.22 = (bf16[12,63,256]{2,1,0:T(8,128)(2,1)S(1)}, bf16[12,63,256]{2,1,0:T(8,128)(2,1)}, u32[]{:S(2)}) copy-start(bf16[12,63,256]{2,1,0:T(8,128)(2,1)} %copy-done.21) | copy-start | bytes 1161220
  130.2 5.8 %copy-start.49 = (f32[1,768,128]{2,0,1:T(1,128)S(1)}, f32[1,768,128]{2,0,1:T(1,128)}, u32[]{:S(2)}) copy-start(f32[1,768,128]{2,0,1:T(1,128)} %fusion.183) | copy-start | bytes 1179652
  141.1 5.6 %copy-start.16 = (bf16[12,63,256]{2,1,0:T(8,128)(2,1)S(1)}, bf16[12,63,256]{2,1,0:T(8,128)(2,1)}, u32[]{:S(2)}) copy-start(bf16[12,63,256]{2,1,0:T(8,128)(2,1)} %copy-done.15) | copy-start | bytes 1161220
  141.1 5.6 %copy-start.18 = (bf16[12,63,256]{2,1,0:T(8,128)(2,1)S(1)}, bf16[12,63,256]{2,1,0:T(8,128)(2,1)}, u32[]{:S(2)}) copy-start(bf16[12,63,256]{2,1,0:T(8,128)(2,1)} %copy-done.17) | copy-start | bytes 1161220
  141.1 5.6 %copy-start.48 = (f32[1,768,128]{2,0,1:T(1,128)S(1)}, f32[1,768,128]{2,0,1:T(1,128)}, u32[]{:S(2)}) copy-start(f32[1,768,128]{2,0,1:T(1,128)} %fusion.187) | copy-start | bytes 1179652
  151.7 5.3 %copy-start.47 = (f32[4]{0:T(128)S(1)}, f32[4]{0:T(128)}, u32[]{:S(2)}) copy-start(f32[4]{0:T(128)} %fusion.191) | copy-start | bytes 52
  151.7 5.5 %copy-start.46 = (f32[4]{0:T(128)S(1)}, f32[4]{0:T(128)}, u32[]{:S(2)}) copy-start(f32[4]{0:T(128)} %fusion.192) | copy-start | bytes 52
  151.7 5.6 %copy-start.45 = (f32[4]{0:T(128)S(1)}, f32[4]{0:T(128)}, u32[]{:S(2)}) copy-start(f32[4]{0:T(128)} %fusion.193) | copy-start | bytes 52
  151.7 5.8 %copy-start.44 = (f32[4]{0:T(128)S(1)}, f32[4]{0:T(128)}, u32[]{:S(2)}) copy-start(f32[4]{0:T(128)} %fusion.194) | copy-start | bytes 52
  227.8 25.9 %collective-permute-start = (bf16[128,4096]{1,0:T(8,128)(2,1)}, bf16[128,4096]{1,0:T(8,128)(2,1)}, u32[]{:S(2)}, u32[]{:S(2)}) collective-permute-start(bf16[128,4096]{1,0:T(8,128)(2,1)} %slice_bitcast_fusion), channel_id=1, source_target_pairs={{0,1},{1,2},{2,3},{3,0},{4,5},{5,6},{6,7},{7,4},{8,9},{9,10},{10,1... | collective-permute-start | bytes 3145736 | tf_op jit(solution)/shard_map/ppermute | solution.py:19
  230.2 177.1 %reduce-scatter.2.cloned.1.call-start = ((), (), s32[]{:S(2)}) async-start(), calls=%async_computation.3 | async-start | bytes 557056 | tf_op jit(solution)/shard_map/reduce_scatter | solution.py:130
  253.7 25.2 %collective-permute-start.1 = (bf16[128,4096]{1,0:T(8,128)(2,1)}, bf16[128,4096]{1,0:T(8,128)(2,1)}, u32[]{:S(2)}, u32[]{:S(2)}) collective-permute-start(bf16[128,4096]{1,0:T(8,128)(2,1)} %collective-permute-done), channel_id=1, source_target_pairs={{0,1},{1,2},{2,3},{3,0},{4,5},{5,6},{6,7},{7,4},{8,9},{9,10},{10,1... | collective-permute-start | bytes 3145736 | tf_op jit(solution)/shard_map/ppermute | solution.py:19
  278.9 24.1 %collective-permute-start.2 = (bf16[128,4096]{1,0:T(8,128)(2,1)}, bf16[128,4096]{1,0:T(8,128)(2,1)}, u32[]{:S(2)}, u32[]{:S(2)}) collective-permute-start(bf16[128,4096]{1,0:T(8,128)(2,1)} %collective-permute-done.1), channel_id=1, source_target_pairs={{0,1},{1,2},{2,3},{3,0},{4,5},{5,6},{6,7},{7,4},{8,9},{9,10},{10,1... | collective-permute-start | bytes 3145736 | tf_op jit(solution)/shard_map/ppermute | solution.py:19
  303.1 2.9 copy-start.2
  332.7 74.7 %copy-start.1 = (bf16[1024,256]{1,0:T(8,128)(2,1)S(1)}, bf16[1024,256]{1,0:T(8,128)(2,1)}, u32[]{:S(2)}) copy-start(bf16[1024,256]{1,0:T(8,128)(2,1)} %param.10) | copy-start | bytes 1572868
Sparse Core Ops, SparseCore 0:
  230.3 32.7 all-gather.1
  343.9 63.3 reduce-scatter.1
